TPU v7x, 128 devices: a whole 4x4x4 slice. The times are simulated.
128 devices in a mesh: seq: 32 (over x, y_hi, z), mp: 4 (over y_lo, core).
Axes of the slice: x: 4, y: 4 (y_hi: 2, y_lo: 2; y = y_hi * 2 + y_lo), z: 4, core: 2. Of those that a mesh axis runs over, the one named last changes fastest.
Arguments:
- hidden_in: bfloat16 [8192, 1536], P('seq', 'mp'), may hold values from -6 to 6
- wq: bfloat16 [1536, 1536], P('seq', 'mp'), may hold values from -1 to 1
- wkv: bfloat16 [1536, 512], P('seq'), may hold values from -0.15625 to 0.15625
- wo: bfloat16 [1536, 1536], P('mp', 'seq'), may hold values from -0.15625 to 0.15625
- lengths: int32 [3], replicated, may hold values from 1 to 6144, 8192 in all
- routes: int32 [8192, 4], P('seq'), may hold values from 0 to 31, all different within a row; in each aligned block of 256 rows (0 to 255, 256 to 511, ...) at most 64 rows name the same one
- gate_logits: float32 [8192, 4], P('seq'), may hold values from -6 to 6
- expert_gate: bfloat16 [32, 768, 1536], P('seq', 'mp'), may hold values from -0.15625 to 0.15625
- expert_up: bfloat16 [32, 768, 1536], P('seq', 'mp'), may hold values from -0.15625 to 0.15625
- expert_down: bfloat16 [32, 768, 1536], P('seq', 'mp'), may hold values from -0.21875 to 0.21875
Outputs:
- layer_out: bfloat16 [8192, 1536], P('seq', 'mp')
Inputs may be any that keep to these rules, and one draw needn't show every extreme that they name: `lengths`: sum to 8192; the longest is exactly 6144. `routes`: a token's 4 experts differ; among the rows of one device no expert is named more than 64 times, a bound that some block reaches.
All inputs are finite; a program needn't handle non-finite values.
Results may differ from a plain program's by a relative error of at most 0.018.
Values may be sent and summed in bfloat16 or wider, within the bound.
No kernel may reach another device: no remote copies, remote signals or barrier semaphores. Data moves between devices by JAX's collectives and lax.ppermute only.
A program may use at most 128 MiB of HBM per device.

v0:
```python
import math
import jax
import jax.numpy as jnp
from jax import lax
from jax.sharding import PartitionSpec as P

D = 1536
HQ = 12
KVH = 2
HD = 128
WINDOW = 4096
ROPE_BASE = 1500000.0
EPSILON = 1e-06


def prompt_ids(index, lengths):
    first_end = lengths[0]
    second_end = lengths[0] + lengths[1]
    prompt = (index >= first_end).astype(jnp.int32) + (index >= second_end).astype(jnp.int32)
    begin = jnp.where(index >= second_end, second_end, jnp.where(index >= first_end, first_end, 0))
    return (prompt, index - begin)


def rotary(values, position):
    half_dim = values.shape[-1] // 2
    freqs = jnp.exp(
        jnp.arange(half_dim, dtype=jnp.float32) * (-2.0 * math.log(ROPE_BASE) / values.shape[-1])
    )
    angles = position.astype(jnp.float32)[:, None] * freqs[None, :]
    cosine = jnp.cos(angles)[:, None, :]
    sine = jnp.sin(angles)[:, None, :]
    front = values[..., :half_dim]
    latter = values[..., half_dim:]
    return jnp.concatenate(
        [front * cosine - latter * sine, latter * cosine + front * sine], axis=-1
    )


def attend(carry, piece, queries, query_index, lengths):
    peak, total, accum = carry
    key_rows = piece[:, 0, :]
    value_rows = piece[:, 1, :].astype(jnp.float32)
    scores = jnp.einsum(
        "hqd,kd->hqk", queries, key_rows, preferred_element_type=jnp.float32
    ) * HD ** (-0.5)
    key_index = jnp.arange(piece.shape[0], dtype=jnp.int32)
    query_prompt, _ = prompt_ids(query_index, lengths)
    key_prompt, _ = prompt_ids(key_index, lengths)
    spacing = query_index[:, None] - key_index[None, :]
    allowed = (
        (query_prompt[:, None] == key_prompt[None, :])
        & (spacing >= 0)
        & (spacing < WINDOW)
        & (key_index[None, :] >= 0)
    )[None]
    masked = jnp.where(allowed, scores, -1e30)
    new_peak = jnp.maximum(peak, jnp.max(masked, axis=-1))
    weights = jnp.where(allowed, jnp.exp(masked - new_peak[..., None]), 0.0)
    total = jnp.sum(weights, axis=-1)
    accum = jnp.einsum("hqk,kd->hqd", weights, value_rows)
    return (new_peak, total, accum)


def local(
    hidden_in, wq, wkv, wo, lengths, routes, gate_logits, expert_gate, expert_up, expert_down
):
    tok_rows = hidden_in.shape[0]
    seq_index = lax.axis_index("seq")
    mp_index = lax.axis_index("mp")
    seq_count = lax.axis_size("seq")
    whole = lax.all_gather(hidden_in, "mp", axis=1, tiled=True)
    whole_f = whole.astype(jnp.float32)
    normed = (
        whole_f * lax.rsqrt(jnp.sum(whole_f * whole_f, axis=-1, keepdims=True) / D + EPSILON)
    ).astype(jnp.bfloat16)
    heads_here = wq.shape[1] // HD
    query_lin = jnp.dot(
        normed, lax.all_gather(wq, "seq", axis=0, tiled=True), preferred_element_type=jnp.float32
    )
    kv_lin = jnp.dot(
        normed, lax.all_gather(wkv, "seq", axis=0, tiled=True), preferred_element_type=jnp.float32
    )
    own_index = seq_index * tok_rows + jnp.arange(tok_rows, dtype=jnp.int32)
    _, own_pos = prompt_ids(own_index, lengths)
    queries = (
        rotary(query_lin.reshape(tok_rows, heads_here, HD), own_pos)
        .astype(jnp.bfloat16)
        .transpose(1, 0, 2)
    )
    kv_group = mp_index * heads_here // (HQ // KVH)
    key_all = kv_lin[:, : KVH * HD].reshape(tok_rows, KVH, HD)
    value_all = kv_lin[:, KVH * HD :].reshape(tok_rows, KVH, HD)
    key_own = rotary(lax.dynamic_slice_in_dim(key_all, kv_group, 1, 1), own_pos)[:, 0, :]
    value_own = lax.dynamic_slice_in_dim(value_all, kv_group, 1, 1)[:, 0, :]
    kv_own = jnp.stack([key_own.astype(jnp.bfloat16), value_own.astype(jnp.bfloat16)], axis=1)
    start_attn = (
        jnp.full((heads_here, tok_rows), -1e30, jnp.float32),
        jnp.zeros((heads_here, tok_rows), jnp.float32),
        jnp.zeros((heads_here, tok_rows, HD), jnp.float32),
    )
    carry = attend(
        start_attn, lax.all_gather(kv_own, "seq", axis=0, tiled=True), queries, own_index, lengths
    )
    _, total, accum = carry
    attended = (
        (accum / total[..., None])
        .transpose(1, 0, 2)
        .reshape(tok_rows, heads_here * HD)
        .astype(jnp.bfloat16)
    )
    partial_out = jnp.dot(
        attended, lax.all_gather(wo, "seq", axis=1, tiled=True), preferred_element_type=jnp.float32
    )
    attn_mine = lax.psum_scatter(
        partial_out.astype(jnp.bfloat16), "mp", scatter_dimension=1, tiled=True
    ).astype(jnp.float32)
    residual = (hidden_in.astype(jnp.float32) + attn_mine).astype(jnp.bfloat16)
    residual_f = residual.astype(jnp.float32)
    square_sum = lax.psum(jnp.sum(residual_f * residual_f, axis=-1), "mp")
    moe_local = (residual_f * lax.rsqrt(square_sum / D + EPSILON)[:, None]).astype(jnp.bfloat16)
    local_experts = expert_gate.shape[0]
    experts = seq_count * local_experts
    top_count = routes.shape[1]
    capacity = 2 * tok_rows * top_count // experts
    flat_ids = routes.reshape(-1)
    one_hot = (flat_ids[:, None] == jnp.arange(experts, dtype=jnp.int32)[None, :]).astype(jnp.int32)
    earlier_count = jnp.sum((jnp.cumsum(one_hot, axis=0) - one_hot) * one_hot, axis=1)
    slot_index = flat_ids * capacity + earlier_count
    source_row = jnp.arange(tok_rows * top_count, dtype=jnp.int32) // top_count
    full_rows = lax.all_gather(moe_local, "mp", axis=1, tiled=True)
    buffer = (
        jnp.zeros((experts * capacity, full_rows.shape[1]), jnp.bfloat16)
        .at[slot_index]
        .set(full_rows[source_row])
    )
    arrived = lax.all_to_all(
        buffer.reshape(experts, capacity, full_rows.shape[1]),
        "seq",
        split_axis=0,
        concat_axis=0,
        tiled=True,
    )
    arrived = arrived.reshape(seq_count, local_experts, capacity, D)
    gate_act = jnp.einsum(
        "secd,efd->secf", arrived, expert_gate, preferred_element_type=jnp.float32
    )
    up_act = jnp.einsum("secd,efd->secf", arrived, expert_up, preferred_element_type=jnp.float32)
    active = (jnp.maximum(gate_act, 0.0) * up_act).astype(jnp.bfloat16)
    partial_expert = jnp.einsum(
        "secf,efd->secd", active, expert_down, preferred_element_type=jnp.float32
    )
    summed = lax.psum_scatter(
        partial_expert.astype(jnp.bfloat16), "mp", scatter_dimension=3, tiled=True
    )
    feature_part = summed.shape[3]
    returned = lax.all_to_all(
        summed.reshape(seq_count * local_experts, capacity, feature_part),
        "seq",
        split_axis=0,
        concat_axis=0,
        tiled=True,
    )
    picked_back = returned.reshape(experts * capacity, feature_part)[slot_index]
    gate_weights = jax.nn.softmax(gate_logits, axis=-1)
    weighted = picked_back.astype(jnp.float32) * gate_weights.reshape(-1)[:, None]
    moe_total = jnp.sum(weighted.reshape(tok_rows, top_count, feature_part), axis=1)
    return (residual_f + moe_total).astype(jnp.bfloat16)


def solution(mesh):
    return jax.shard_map(
        local,
        mesh=mesh,
        in_specs=(
            P("seq", "mp"),
            P("seq", "mp"),
            P("seq", None),
            P("mp", "seq"),
            P(),
            P("seq", None),
            P("seq", None),
            P("seq", "mp", None),
            P("seq", "mp", None),
            P("seq", "mp", None),
        ),
        out_specs=P("seq", "mp"),
        check_vma=False,
    )
```

profile of v0, /device:TPU:0, one launch (start us, length us, event | category | flops | bytes accessed | tf_op | source)
XLA Modules:
  0.0 610.1 jit_solution(7796226806283322392)
XLA Ops:
  11.4 9.0 %all_gather.18 = bf16[256,1536]{1,0:T(8,128)(2,1)S(1)} all-gather(bf16[256,384]{1,0:T(8,128)(2,1)} %param.10), channel_id=1, replica_groups=mesh['seq'=32,'mp'=4] {'mp'}, dimensions={1}, use_global_device_ids=true | all-gather | bytes 983040 | tf_op jit(solution)/shard_map/all_gather | solution.py:71
  20.7 60.8 %all-gather.7.cloned.1.call-done = bf16[1536,512]{1,0:T(8,128)(2,1)} async-done(((bf16[48,512]{1,0:T(8,128)(2,1)}), bf16[1536,512]{1,0:T(8,128)(2,1)}) %all-gather.7.cloned.1.call-update) | async-done | bytes 1572880 | tf_op jit(solution)/shard_map/all_gather | solution.py:81
  90.7 57.7 %all-gather.5.cloned.1.call-done = bf16[1536,384]{1,0:T(8,128)(2,1)} async-done(((bf16[48,384]{1,0:T(8,128)(2,1)}), bf16[1536,384]{1,0:T(8,128)(2,1)}) %all-gather.5.cloned.1.call-update) | async-done | bytes 1179664 | tf_op jit(solution)/shard_map/all_gather | solution.py:78
  154.2 74.4 %all-gather.9.cloned.1.call-done = bf16[8192,2,128]{0,2,1:T(8,128)(2,1)} async-done(((bf16[256,2,128]{0,2,1:T(8,128)(2,1)}), bf16[8192,2,128]{0,2,1:T(8,128)(2,1)}) %all-gather.9.cloned.1.call-update) | async-done | bytes 4194320 | tf_op jit(solution)/shard_map/all_gather | solution.py:102
  228.5 12.2 %fusion = (f32[3,256]{1,0:T(4,128)S(1)}, f32[3,256,8192]{2,1,0:T(8,128)}) fusion(pred[256,8192]{1,0:T(8,128)(4,1)S(1)} %fusion.11, bf16[8192,2,128]{0,2,1:T(8,128)(2,1)} %all-gather.9.cloned.1.call-done, bf16[256,3,64]{2,0,1:T(8,128)(2,1)} %get-tuple-element.6, bf16[256,3,64]{2,0,1:T(8,128)(2,1)} %get-tuple-element.5), kind=kOutput, calls=%fused_computation.5 | convolution fusion | flops 1629879552 | bytes 29756416 | tf_op jit(solution)/shard_map/hqd,kd->hqk/dot_general | solution.py:43
  240.8 12.5 %fusion.1 = f32[3,256]{1,0:T(4,128)S(1)} fusion(f32[3,256,8192]{2,1,0:T(8,128)} %get-tuple-element.16, f32[3,256]{1,0:T(4,128)S(1)} %broadcast_maximum_fusion, pred[256,8192]{1,0:T(8,128)(4,1)S(1)} %fusion.11), kind=kLoop, calls=%fused_computation.6 | loop fusion | flops 31456512 | bytes 27269120 | tf_op jit(solution)/shard_map/reduce_sum | solution.py:59
  253.3 11.8 %fusion.20 = bf16[256,3,128]{0,2,1:T(8,128)(2,1)S(1)} fusion(bf16[8192,2,128]{0,2,1:T(8,128)(2,1)S(1)} %copy-done.5, f32[3,256,8192]{2,1,0:T(8,128)} %get-tuple-element.16, f32[3,256]{1,0:T(4,128)S(1)} %broadcast_maximum_fusion, pred[256,8192]{1,0:T(8,128)(4,1)S(1)} %fusion.11, f32[256,3]{0,1:T(4,128)S(1)} %bitcast.108), kind=kOutput, calls=%fused_computation.34 | convolution fusion | flops 1635975168 | bytes 29564928 | tf_op jit(solution)/shard_map/hqk,kd->hqd/dot_general | solution.py:60
  265.1 33.9 %all-gather.11.cloned.1.call-done = bf16[384,1536]{0,1:T(8,128)(2,1)} async-done(((bf16[384,48]{0,1:T(8,128)(2,1)}), bf16[384,1536]{0,1:T(8,128)(2,1)}) %all-gather.11.cloned.1.call-update) | async-done | bytes 1179664 | tf_op jit(solution)/shard_map/all_gather | solution.py:112
  302.7 9.0 %reduce-window.6 = s32[32,8,128]{2,1,0:T(8,128)S(1)} reduce-window(s32[32,8,128]{2,1,0:T(8,128)S(1)} %fusion.38, s32[]{:T(128)} %constant.26.clone.1), window={size=1x1x128 pad=0_0x0_0x127_0}, to_apply=%region_4.5 | reduce-window | flops 4161536 | bytes 262148 | tf_op jit(solution)/shard_map/reduce-window
  312.6 5.7 reduce-scatter.7.cloned.1.call-done
  319.5 5.9 psum.7
  325.5 8.7 %all_gather.23 = bf16[256,1536]{1,0:T(8,128)(2,1)S(1)} all-gather(bf16[256,384]{1,0:T(8,128)(2,1)S(1)} %fusion.27), channel_id=1, replica_groups=mesh['seq'=32,'mp'=4] {'mp'}, dimensions={1}, use_global_device_ids=true | all-gather | bytes 983040 | tf_op jit(solution)/shard_map/all_gather | solution.py:130
  334.3 19.7 %scatter_custom_fusion = bf16[2048,1536]{1,0:T(8,128)(2,1)} fusion(s32[1024]{0:T(1024)S(1)} %bitcast.105, bf16[256,1536]{1,0:T(8,128)(2,1)S(1)} %all_gather.23, s32[1024]{0:T(1024)S(1)} %broadcast_clamp_fusion.1, bf16[]{:T(256)} %constant.75.clone.1), kind=kCustom, calls=%fused_computation.19 | custom fusion | bytes 6291458 | tf_op jit(solution)/shard_map/scatter | solution.py:134
  354.0 84.0 %all_to_all.10 = bf16[32,64,1536]{2,1,0:T(8,128)(2,1)S(1)} all-to-all(bf16[32,64,1536]{2,1,0:T(8,128)(2,1)} %bitcast.93), channel_id=1, replica_groups=mesh['seq'=32,'mp'=4] {'seq'}, dimensions={0} | all-to-all | bytes 12582912 | tf_op jit(solution)/shard_map/all_to_all | solution.py:136
  440.6 3.2 fusion.24
  443.8 12.3 %convert_bitcast_fusion = bf16[32,1,64,1536]{3,2,0,1:T(8,128)(2,1)} fusion(f32[32,64,192]{2,1,0:T(8,128)} %fusion.24, bf16[32,64,1536]{2,1,0:T(8,128)(2,1)} %copy-done.1, bf16[1,192,1536]{2,1,0:T(8,128)(2,1)S(1)} %copy-done, bf16[1,192,1536]{2,1,0:T(8,128)(2,1)S(1)} %copy-done.7), kind=kOutput, calls=%fused_computation.18 | convolution fusion | flops 2420244480 | bytes 15335424 | tf_op jit(solution)/shard_map/secf,efd->secd/dot_general | solution.py:149
  456.1 18.4 %copy.58 = bf16[32,1,64,1536]{2,0,1,3:T(8,128)(2,1)} copy(bf16[32,1,64,1536]{3,2,0,1:T(8,128)(2,1)} %convert_bitcast_fusion) | data formatting | bytes 12582912
  474.5 17.9 %reshape.397 = bf16[1536,2048]{1,0:T(8,128)(2,1)} reshape(bf16[1536,1,32,64]{3,2,1,0:T(8,128)(2,1)} %bitcast.91) | data formatting | bytes 12582912
  492.4 60.4 %reduce-scatter.9.cloned.1.call-done = bf16[384,2048]{1,0:T(8,128)(2,1)} async-done(((bf16[1536,2048]{1,0:T(8,128)(2,1)}), bf16[384,2048]{1,0:T(8,128)(2,1)}) %reduce-scatter.9.cloned.1.call-update) | async-done | bytes 1572880
  552.8 5.7 reshape.398
  558.5 5.5 copy.59
  564.0 9.4 %all-to-all-start.1 = ((bf16[32,64,384]{2,1,0:T(8,128)(2,1)}), bf16[32,64,384]{2,1,0:T(8,128)(2,1)S(1)}, u32[]{:S(2)}, u32[]{:S(2)}) async-start(bf16[32,64,384]{2,1,0:T(8,128)(2,1)} %bitcast.95), calls=%async_computation.1 | async-start | bytes 3145728 | tf_op jit(solution)/shard_map/all_to_all | solution.py:156
  573.6 23.2 %all-to-all-done.1 = bf16[32,64,384]{2,1,0:T(8,128)(2,1)S(1)} async-done(((bf16[32,64,384]{2,1,0:T(8,128)(2,1)}), bf16[32,64,384]{2,1,0:T(8,128)(2,1)S(1)}, u32[]{:S(2)}, u32[]{:S(2)}) %all-to-all-start.1) | async-done | bytes 1572896 | tf_op jit(solution)/shard_map/all_to_all | solution.py:156
  596.8 3.9 gather_fusion
  (82 shorter events, 29.4 us)
Async XLA Ops:
  6.5 437.3 %copy-start = (bf16[1,192,1536]{2,1,0:T(8,128)(2,1)S(1)}, bf16[1,192,1536]{2,1,0:T(8,128)(2,1)}, u32[]{:S(2)}) copy-start(bf16[1,192,1536]{2,1,0:T(8,128)(2,1)} %param.19) | copy-start | bytes 1769476
  6.5 74.9 %all-gather.7.cloned.1.call-start = ((), (), s32[]{:S(2)}) async-start(), calls=%async_computation.5 | async-start | bytes 1622016 | tf_op jit(solution)/shard_map/all_gather | solution.py:81
  7.3 141.2 %all-gather.5.cloned.1.call-start = ((), (), s32[]{:S(2)}) async-start(), calls=%async_computation.4 | async-start | bytes 1216512 | tf_op jit(solution)/shard_map/all_gather | solution.py:78
  8.0 220.5 %all-gather.9.cloned.1.call-start = ((), (), s32[]{:S(2)}) async-start(), calls=%async_computation.6 | async-start | bytes 4325376 | tf_op jit(solution)/shard_map/all_gather | solution.py:102
  84.8 214.2 %all-gather.11.cloned.1.call-start = ((), (), s32[]{:S(2)}) async-start(), calls=%async_computation.7 | async-start | bytes 1216512 | tf_op jit(solution)/shard_map/all_gather | solution.py:112
  85.4 232.9 %reduce-scatter.7.cloned.1.call-start = ((), (), s32[]{:S(2)}) async-start(), calls=%async_computation.8 | async-start | bytes 983040
  240.8 12.5 %copy-start.5 = (bf16[8192,2,128]{0,2,1:T(8,128)(2,1)S(1)}, bf16[8192,2,128]{0,2,1:T(8,128)(2,1)}, u32[]{:S(2)}) copy-start(bf16[8192,2,128]{0,2,1:T(8,128)(2,1)} %all-gather.9.cloned.1.call-done) | copy-start | bytes 12582916
  265.1 37.2 %copy-start.4 = (s32[256,4]{0,1:T(4,128)S(1)}, s32[256,4]{0,1:T(4,128)}, u32[]{:S(2)}) copy-start(s32[256,4]{0,1:T(4,128)} %param.15) | copy-start | bytes 12292
  265.1 54.2 %copy-start.2 = (bf16[256,384]{1,0:T(8,128)(2,1)S(1)}, bf16[256,384]{1,0:T(8,128)(2,1)}, u32[]{:S(2)}) copy-start(bf16[256,384]{1,0:T(8,128)(2,1)} %param.10) | copy-start | bytes 589828
  302.1 250.7 %reduce-scatter.9.cloned.1.call-start = ((), (), s32[]{:S(2)}) async-start(), calls=%async_computation.9 | async-start | bytes 7864320
  354.0 86.7 %copy-start.6 = (bf16[1,192,1536]{2,1,0:T(8,128)(2,1)S(1)}, bf16[1,192,1536]{2,1,0:T(8,128)(2,1)}, u32[]{:S(2)}) copy-start(bf16[1,192,1536]{2,1,0:T(8,128)(2,1)} %param.17) | copy-start | bytes 1769476
  438.0 2.7 copy-start.1
  440.6 3.2 copy-start.7
  558.5 14.8 %copy-start.3 = (f32[256,4]{0,1:T(4,128)S(1)}, f32[256,4]{0,1:T(4,128)}, u32[]{:S(2)}) copy-start(f32[256,4]{0,1:T(4,128)} %param.16) | copy-start | bytes 12292
  564.0 32.8 %all-to-all-start.1 = ((bf16[32,64,384]{2,1,0:T(8,128)(2,1)}), bf16[32,64,384]{2,1,0:T(8,128)(2,1)S(1)}, u32[]{:S(2)}, u32[]{:S(2)}) async-start(bf16[32,64,384]{2,1,0:T(8,128)(2,1)} %bitcast.95), calls=%async_computation.1 | async-start | bytes 3145728 | tf_op jit(solution)/shard_map/all_to_all | solution.py:156
Sparse Core Ops, SparseCore 0:
  10.4 71.0 all-gather.6
  84.4 63.9 all-gather.4
  151.3 77.2 all-gather.8
  231.4 67.6 all-gather.10
  302.2 15.9 reduce-scatter.6
  492.6 60.2 reduce-scatter.8
where the time goes:
time: 620 us; the launch traced here: 610 us
  waiting for transfers between devices  318 us (51%)
  blocking collectives  108 us (17%)
  local copies, waits for them, and re-layouts  81 us (13%)
  matrix products  45.3 us (7%)
  other arithmetic  32.8 us (5%)
  between operations  15.5 us (2%)
  starting transfers between devices  9.75 us (2%)
    all_to_all x1, blocking collectives, local(): lax.all_to_all(buffer.reshape(experts, capacity, full_rows.shape[1]), 'se...  84 us
    all_gather x1, waiting for transfers between devices, local(): lax.all_gather(kv_own, 'seq', axis=0, tiled=True)  74.4 us
    unnamed x8, waiting for transfers between devices  68 us
    all_gather x1, waiting for transfers between devices, local(): lax.all_gather(wkv, 'seq', axis=0, tiled=True)  60.8 us
    all_gather x1, waiting for transfers between devices, local(): lax.all_gather(wq, 'seq', axis=0, tiled=True)  57.7 us
    unnamed x25, local copies, waits for them, and re-layouts  53.8 us
    all_gather x1, waiting for transfers between devices, local(): lax.all_gather(wo, 'seq', axis=1, tiled=True)  33.9 us
    all_to_all x1, waiting for transfers between devices, local(): lax.all_to_all(summed.reshape(seq_count * local_experts, capacity, featur...  23.2 us
  transfers between devices with their start and end apart: 7, of which 7 were waited for; matrix products, arithmetic and copies ran while one was open for 10% of the time, Pallas kernels for 0%

commit v1 on v0

--- a/solution.py
+++ b/solution.py
@@ -1,3 +1,4 @@
+import functools
 import math
 import jax
 import jax.numpy as jnp
@@ -11,6 +12,18 @@
 WINDOW = 4096
 ROPE_BASE = 1500000.0
 EPSILON = 1e-06
+
+
+def hubs_fill(here_x, across):
+    return jnp.concatenate(
+        lax.all_to_all(
+            jnp.stack(tuple((here_x for _ in range(lax.axis_size(across)))), 0), across, 0, 0
+        ),
+        0,
+    )
+
+
+lay_cells = functools.partial(hubs_fill, across="seq")
 
 
 def prompt_ids(index, lengths):
@@ -77,9 +90,7 @@
     query_lin = jnp.dot(
         normed, lax.all_gather(wq, "seq", axis=0, tiled=True), preferred_element_type=jnp.float32
     )
-    kv_lin = jnp.dot(
-        normed, lax.all_gather(wkv, "seq", axis=0, tiled=True), preferred_element_type=jnp.float32
-    )
+    kv_lin = jnp.dot(normed, lay_cells(wkv), preferred_element_type=jnp.float32)
     own_index = seq_index * tok_rows + jnp.arange(tok_rows, dtype=jnp.int32)
     _, own_pos = prompt_ids(own_index, lengths)
     queries = (

time: 620 us -> 556 us (0.90)
  waiting for transfers between devices: 318 us -> 237 us
  starting transfers between devices: 9.75 us -> 20.9 us
  blocking collectives: 108 us -> 119 us
    all_gather x1 -> x0, waiting for transfers between devices: 60.8 us -> none  [local(): lax.all_gather(wkv, 'seq', axis=0, tiled=True)]
    all_gather x1, waiting for transfers between devices: 57.7 us -> 37.9 us  [local(): lax.all_gather(wq, 'seq', axis=0, tiled=True)]
    all_gather x1, blocking collectives: 8.98 us -> 20.6 us  [local(): whole = lax.all_gather(hidden_in, 'mp', axis=1, tiled=True)]
    all_to_all x0 -> x1, starting transfers between devices: none -> 10.9 us  [hubs_fill(): lax.all_to_all(jnp.stack(tuple((here_x for _ in range(lax.axis_size(acros...]
    unnamed x8 -> x7, waiting for transfers between devices: 68 us -> 67.8 us
    unnamed x25 -> x29, local copies, waits for them, and re-layouts: 53.8 us -> 53.8 us
  transfers between devices with their start and end apart: 7 -> 7, of which waited for: 7 -> 6; matrix products, arithmetic and copies ran while one was open for 10% -> 11% of each run, Pallas kernels for 0% -> 0%
where the time goes in v1:
time: 556 us; the launch traced here: 552 us
  waiting for transfers between devices  237 us (43%)
  blocking collectives  119 us (21%)
  local copies, waits for them, and re-layouts  82.4 us (15%)
  matrix products  43.9 us (8%)
  other arithmetic  32.8 us (6%)
  starting transfers between devices  20.9 us (4%)
  between operations  15.1 us (3%)
    all_to_all x1, blocking collectives, local(): lax.all_to_all(buffer.reshape(experts, capacity, full_rows.shape[1]), 'se...  83.9 us
    all_gather x1, waiting for transfers between devices, local(): lax.all_gather(kv_own, 'seq', axis=0, tiled=True)  74.4 us
    unnamed x7, waiting for transfers between devices  67.8 us
    unnamed x29, local copies, waits for them, and re-layouts  53.8 us
    all_gather x1, waiting for transfers between devices, local(): lax.all_gather(wq, 'seq', axis=0, tiled=True)  37.9 us
    all_gather x1, waiting for transfers between devices, local(): lax.all_gather(wo, 'seq', axis=1, tiled=True)  34.1 us
    all_to_all x1, waiting for transfers between devices, local(): lax.all_to_all(summed.reshape(seq_count * local_experts, capacity, featur...  23.2 us
    all_gather x1, blocking collectives, local(): whole = lax.all_gather(hidden_in, 'mp', axis=1, tiled=True)  20.6 us
  transfers between devices with their start and end apart: 7, of which 6 were waited for; matrix products, arithmetic and copies ran while one was open for 11% of the time, Pallas kernels for 0%

profile of v1, /device:TPU:0, one launch (start us, length us, event | category | flops | bytes accessed | tf_op | source)
XLA Modules:
  0.0 551.7 jit_solution(7780043015228748415)
XLA Ops:
  9.4 10.9 %all-to-all-start = ((bf16[32,48,512]{2,1,0:T(8,128)(2,1)}), bf16[32,48,512]{2,1,0:T(8,128)(2,1)S(1)}, u32[]{:S(2)}, u32[]{:S(2)}) async-start(bf16[32,48,512]{2,1,0:T(8,128)(2,1)} %stack.4), calls=%async_computation | async-start | bytes 3145728 | tf_op jit(solution)/shard_map/all_to_all | solution.py:19
  23.0 20.6 %all_gather.15 = bf16[256,1536]{1,0:T(8,128)(2,1)S(1)} all-gather(bf16[256,384]{1,0:T(8,128)(2,1)S(1)} %copy-done.2), channel_id=1, replica_groups=mesh['seq'=32,'mp'=4] {'mp'}, dimensions={1}, use_global_device_ids=true | all-gather | bytes 983040 | tf_op jit(solution)/shard_map/all_gather | solution.py:84
  52.3 37.9 %all-gather.4.cloned.1.call-done = bf16[1536,384]{1,0:T(8,128)(2,1)} async-done(((bf16[48,384]{1,0:T(8,128)(2,1)}), bf16[1536,384]{1,0:T(8,128)(2,1)}) %all-gather.4.cloned.1.call-update) | async-done | bytes 1179664 | tf_op jit(solution)/shard_map/all_gather | solution.py:91
  95.9 74.4 %all-gather.6.cloned.1.call-done = bf16[8192,2,128]{0,2,1:T(8,128)(2,1)} async-done(((bf16[256,2,128]{0,2,1:T(8,128)(2,1)}), bf16[8192,2,128]{0,2,1:T(8,128)(2,1)}) %all-gather.6.cloned.1.call-update) | async-done | bytes 4194320 | tf_op jit(solution)/shard_map/all_gather | solution.py:113
  170.2 12.2 %fusion = (f32[3,256]{1,0:T(4,128)S(1)}, f32[3,256,8192]{2,1,0:T(8,128)}) fusion(pred[256,8192]{1,0:T(8,128)(4,1)S(1)} %fusion.11, bf16[8192,2,128]{0,2,1:T(8,128)(2,1)} %all-gather.6.cloned.1.call-done, bf16[256,3,64]{2,0,1:T(8,128)(2,1)} %get-tuple-element.6, bf16[256,3,64]{2,0,1:T(8,128)(2,1)} %get-tuple-element.5), kind=kOutput, calls=%fused_computation.5 | convolution fusion | flops 1629879552 | bytes 29756416 | tf_op jit(solution)/shard_map/hqd,kd->hqk/dot_general | solution.py:56
  182.4 12.5 %fusion.1 = f32[3,256]{1,0:T(4,128)S(1)} fusion(f32[3,256,8192]{2,1,0:T(8,128)} %get-tuple-element.16, f32[3,256]{1,0:T(4,128)S(1)} %broadcast_maximum_fusion, pred[256,8192]{1,0:T(8,128)(4,1)S(1)} %fusion.11), kind=kLoop, calls=%fused_computation.6 | loop fusion | flops 31456512 | bytes 27269120 | tf_op jit(solution)/shard_map/reduce_sum | solution.py:72
  195.0 11.8 %fusion.20 = bf16[256,3,128]{0,2,1:T(8,128)(2,1)S(1)} fusion(bf16[8192,2,128]{0,2,1:T(8,128)(2,1)S(1)} %copy-done.7, f32[3,256,8192]{2,1,0:T(8,128)} %get-tuple-element.16, f32[3,256]{1,0:T(4,128)S(1)} %broadcast_maximum_fusion, pred[256,8192]{1,0:T(8,128)(4,1)S(1)} %fusion.11, f32[256,3]{0,1:T(4,128)S(1)} %bitcast.110), kind=kOutput, calls=%fused_computation.34 | convolution fusion | flops 1635975168 | bytes 29564928 | tf_op jit(solution)/shard_map/hqk,kd->hqd/dot_general | solution.py:73
  206.8 34.1 %all-gather.8.cloned.1.call-done = bf16[384,1536]{0,1:T(8,128)(2,1)} async-done(((bf16[384,48]{0,1:T(8,128)(2,1)}), bf16[384,1536]{0,1:T(8,128)(2,1)}) %all-gather.8.cloned.1.call-update) | async-done | bytes 1179664 | tf_op jit(solution)/shard_map/all_gather | solution.py:123
  244.4 9.0 %reduce-window.6 = s32[32,8,128]{2,1,0:T(8,128)S(1)} reduce-window(s32[32,8,128]{2,1,0:T(8,128)S(1)} %fusion.38, s32[]{:T(128)} %constant.26.clone.1), window={size=1x1x128 pad=0_0x0_0x127_0}, to_apply=%region_4.5 | reduce-window | flops 4161536 | bytes 262148 | tf_op jit(solution)/shard_map/reduce-window
  254.2 5.9 %reduce-scatter.7.cloned.1.call-done = bf16[384,256]{1,0:T(8,128)(2,1)} async-done(((bf16[1536,256]{1,0:T(8,128)(2,1)}), bf16[384,256]{1,0:T(8,128)(2,1)}) %reduce-scatter.7.cloned.1.call-update) | async-done | bytes 196624
  261.4 6.0 %psum.7 = f32[256]{0:T(256)S(1)} all-reduce(f32[256]{0:T(256)S(1)} %fusion.26), channel_id=1, replica_groups=mesh['seq'=32,'mp'=4] {'mp'}, use_global_device_ids=true, to_apply=%region_8.9 | all-reduce | flops 256 | bytes 2048 | tf_op jit(solution)/shard_map/psum | solution.py:130
  267.5 8.9 %all_gather.19 = bf16[256,1536]{1,0:T(8,128)(2,1)S(1)} all-gather(bf16[256,384]{1,0:T(8,128)(2,1)S(1)} %fusion.27), channel_id=1, replica_groups=mesh['seq'=32,'mp'=4] {'mp'}, dimensions={1}, use_global_device_ids=true | all-gather | bytes 983040 | tf_op jit(solution)/shard_map/all_gather | solution.py:141
  276.4 19.7 %scatter_custom_fusion = bf16[2048,1536]{1,0:T(8,128)(2,1)} fusion(s32[1024]{0:T(1024)S(1)} %bitcast.107, bf16[256,1536]{1,0:T(8,128)(2,1)S(1)} %all_gather.19, s32[1024]{0:T(1024)S(1)} %broadcast_clamp_fusion.1, bf16[]{:T(256)} %constant.75.clone.1), kind=kCustom, calls=%fused_computation.19 | custom fusion | bytes 6291458 | tf_op jit(solution)/shard_map/scatter | solution.py:145
  296.1 83.9 %all_to_all.15 = bf16[32,64,1536]{2,1,0:T(8,128)(2,1)S(1)} all-to-all(bf16[32,64,1536]{2,1,0:T(8,128)(2,1)} %bitcast.94), channel_id=1, replica_groups=mesh['seq'=32,'mp'=4] {'seq'}, dimensions={0} | all-to-all | bytes 12582912 | tf_op jit(solution)/shard_map/all_to_all | solution.py:147
  382.6 3.2 fusion.24
  385.8 12.3 %convert_bitcast_fusion = bf16[32,1,64,1536]{3,2,0,1:T(8,128)(2,1)} fusion(f32[32,64,192]{2,1,0:T(8,128)} %fusion.24, bf16[32,64,1536]{2,1,0:T(8,128)(2,1)} %copy-done.1, bf16[1,192,1536]{2,1,0:T(8,128)(2,1)S(1)} %copy-done, bf16[1,192,1536]{2,1,0:T(8,128)(2,1)S(1)} %copy-done.9), kind=kOutput, calls=%fused_computation.18 | convolution fusion | flops 2420244480 | bytes 15335424 | tf_op jit(solution)/shard_map/secf,efd->secd/dot_general | solution.py:160
  398.1 18.4 %copy.58 = bf16[32,1,64,1536]{2,0,1,3:T(8,128)(2,1)} copy(bf16[32,1,64,1536]{3,2,0,1:T(8,128)(2,1)} %convert_bitcast_fusion) | data formatting | bytes 12582912
  416.5 17.9 %reshape.403 = bf16[1536,2048]{1,0:T(8,128)(2,1)} reshape(bf16[1536,1,32,64]{3,2,1,0:T(8,128)(2,1)} %bitcast.92) | data formatting | bytes 12582912
  434.4 60.5 %reduce-scatter.9.cloned.1.call-done = bf16[384,2048]{1,0:T(8,128)(2,1)} async-done(((bf16[1536,2048]{1,0:T(8,128)(2,1)}), bf16[384,2048]{1,0:T(8,128)(2,1)}) %reduce-scatter.9.cloned.1.call-update) | async-done | bytes 1572880
  494.9 5.7 %reshape.404 = bf16[384,1,32,64]{3,2,1,0:T(8,128)(2,1)} reshape(bf16[384,2048]{1,0:T(8,128)(2,1)} %reduce-scatter.9.cloned.1.call-done) | data formatting | bytes 3145728
  500.6 5.5 copy.59
  506.1 9.4 %all-to-all-start.2 = ((bf16[32,64,384]{2,1,0:T(8,128)(2,1)}), bf16[32,64,384]{2,1,0:T(8,128)(2,1)S(1)}, u32[]{:S(2)}, u32[]{:S(2)}) async-start(bf16[32,64,384]{2,1,0:T(8,128)(2,1)} %bitcast.96), calls=%async_computation.2 | async-start | bytes 3145728 | tf_op jit(solution)/shard_map/all_to_all | solution.py:167
  515.7 23.2 %all-to-all-done.2 = bf16[32,64,384]{2,1,0:T(8,128)(2,1)S(1)} async-done(((bf16[32,64,384]{2,1,0:T(8,128)(2,1)}), bf16[32,64,384]{2,1,0:T(8,128)(2,1)S(1)}, u32[]{:S(2)}, u32[]{:S(2)}) %all-to-all-start.2) | async-done | bytes 1572896 | tf_op jit(solution)/shard_map/all_to_all | solution.py:167
  538.9 3.9 gather_fusion
  (86 shorter events, 29.1 us)
Async XLA Ops:
  6.5 379.3 %copy-start = (bf16[1,192,1536]{2,1,0:T(8,128)(2,1)S(1)}, bf16[1,192,1536]{2,1,0:T(8,128)(2,1)}, u32[]{:S(2)}) copy-start(bf16[1,192,1536]{2,1,0:T(8,128)(2,1)} %param.19) | copy-start | bytes 1769476
  6.5 13.8 %copy-start.6 = (s32[3]{0:T(128)S(1)}, s32[3]{0:T(128)}, u32[]{:S(2)}) copy-start(s32[3]{0:T(128)} %param.14) | copy-start | bytes 40
  6.5 16.4 %copy-start.2 = (bf16[256,384]{1,0:T(8,128)(2,1)S(1)}, bf16[256,384]{1,0:T(8,128)(2,1)}, u32[]{:S(2)}) copy-start(bf16[256,384]{1,0:T(8,128)(2,1)} %param.10) | copy-start | bytes 589828
  6.5 83.6 %all-gather.4.cloned.1.call-start = ((), (), s32[]{:S(2)}) async-start(), calls=%async_computation.5 | async-start | bytes 1216512 | tf_op jit(solution)/shard_map/all_gather | solution.py:91
  9.4 34.4 %all-to-all-start = ((bf16[32,48,512]{2,1,0:T(8,128)(2,1)}), bf16[32,48,512]{2,1,0:T(8,128)(2,1)S(1)}, u32[]{:S(2)}, u32[]{:S(2)}) async-start(bf16[32,48,512]{2,1,0:T(8,128)(2,1)} %stack.4), calls=%async_computation | async-start | bytes 3145728 | tf_op jit(solution)/shard_map/all_to_all | solution.py:19
  20.3 149.9 %all-gather.6.cloned.1.call-start = ((), (), s32[]{:S(2)}) async-start(), calls=%async_computation.6 | async-start | bytes 4325376 | tf_op jit(solution)/shard_map/all_gather | solution.py:113
  45.7 195.1 %all-gather.8.cloned.1.call-start = ((), (), s32[]{:S(2)}) async-start(), calls=%async_computation.7 | async-start | bytes 1216512 | tf_op jit(solution)/shard_map/all_gather | solution.py:123
  46.5 213.6 %reduce-scatter.7.cloned.1.call-start = ((), (), s32[]{:S(2)}) async-start(), calls=%async_computation.8 | async-start | bytes 983040
  182.4 12.5 %copy-start.7 = (bf16[8192,2,128]{0,2,1:T(8,128)(2,1)S(1)}, bf16[8192,2,128]{0,2,1:T(8,128)(2,1)}, u32[]{:S(2)}) copy-start(bf16[8192,2,128]{0,2,1:T(8,128)(2,1)} %all-gather.6.cloned.1.call-done) | copy-start | bytes 12582916
  206.8 37.2 %copy-start.5 = (s32[256,4]{0,1:T(4,128)S(1)}, s32[256,4]{0,1:T(4,128)}, u32[]{:S(2)}) copy-start(s32[256,4]{0,1:T(4,128)} %param.15) | copy-start | bytes 12292
  206.8 54.4 %copy-start.3 = (bf16[256,384]{1,0:T(8,128)(2,1)S(1)}, bf16[256,384]{1,0:T(8,128)(2,1)}, u32[]{:S(2)}) copy-start(bf16[256,384]{1,0:T(8,128)(2,1)} %param.10) | copy-start | bytes 589828
  243.9 251.0 %reduce-scatter.9.cloned.1.call-start = ((), (), s32[]{:S(2)}) async-start(), calls=%async_computation.9 | async-start | bytes 7864320
  296.1 86.5 %copy-start.8 = (bf16[1,192,1536]{2,1,0:T(8,128)(2,1)S(1)}, bf16[1,192,1536]{2,1,0:T(8,128)(2,1)}, u32[]{:S(2)}) copy-start(bf16[1,192,1536]{2,1,0:T(8,128)(2,1)} %param.17) | copy-start | bytes 1769476
  380.0 2.7 copy-start.1
  382.6 3.2 copy-start.9
  500.6 14.9 %copy-start.4 = (f32[256,4]{0,1:T(4,128)S(1)}, f32[256,4]{0,1:T(4,128)}, u32[]{:S(2)}) copy-start(f32[256,4]{0,1:T(4,128)} %param.16) | copy-start | bytes 12292
  506.1 32.8 %all-to-all-start.2 = ((bf16[32,64,384]{2,1,0:T(8,128)(2,1)}), bf16[32,64,384]{2,1,0:T(8,128)(2,1)S(1)}, u32[]{:S(2)}, u32[]{:S(2)}) async-start(bf16[32,64,384]{2,1,0:T(8,128)(2,1)} %bitcast.96), calls=%async_computation.2 | async-start | bytes 3145728 | tf_op jit(solution)/shard_map/all_to_all | solution.py:167
Sparse Core Ops, SparseCore 0:
  10.3 79.8 all-gather.3
  92.9 77.2 all-gather.5
  173.2 67.6 all-gather.7
  244.1 16.0 reduce-scatter.6
  434.6 60.3 reduce-scatter.8
